TPU v7x, 32 devices: a whole 2x2x4 slice. The times are simulated.
32 devices in a mesh: dp: 8 (over y, x, core), expert: 4 (over z).
Axes of the slice: x: 2, y: 2, z: 4, core: 2. Of those that a mesh axis runs over, the one named last changes fastest.
Arguments:
- hidden: bfloat16 [2, 512, 2880], P(None, ('dp', 'expert')), may hold values from -1.5 to 1.5
- norm_gain: float32 [2880], replicated, may hold values from 0.1 to 1.9
- router: bfloat16 [2880, 64], replicated, may hold values from -0.078125 to 0.078125
- routes: int32 [2, 512, 4], P(None, ('dp', 'expert')), may hold values from 0 to 63, all different within a row; in each aligned block of 16 rows (0 to 15, 16 to 31, ..., all dimensions but the last counted through in order) at most 2 rows name the same one
- w_gate: bfloat16 [64, 2880, 2048], P('expert', None, 'dp'), may hold values from -0.109375 to 0.109375
- w_up: bfloat16 [64, 2880, 2048], P('expert', None, 'dp'), may hold values from -0.109375 to 0.109375
- w_down: bfloat16 [64, 2048, 2880], P('expert', 'dp'), may hold values from -0.125 to 0.125
- queries: bfloat16 [2, 512, 4096], P(None, ('dp', 'expert')), may hold values from -5.5 to 5.5
- new_key: bfloat16 [2, 512, 512], P(None, ('dp', 'expert')), may hold values from -8 to 8
- new_value: bfloat16 [2, 512, 512], P(None, ('dp', 'expert')), may hold values from -6 to 6
- key_pages: bfloat16 [256, 4, 16, 512], P(('dp', 'expert')), may hold values from -6 to 6
- value_pages: bfloat16 [256, 4, 16, 512], P(('dp', 'expert')), may hold values from -6 to 6
- page_counts: int32 [32, 16], P(('dp', 'expert')), may hold values from 1 to 10, 32 in all within a row
- page_order: int32 [32, 32], P(('dp', 'expert')), may hold values from 0 to 31, each once within a row
Outputs:
- context: bfloat16 [2, 512, 4096], P(None, ('dp', 'expert'))
- layer_out: bfloat16 [2, 512, 2880], P(None, ('dp', 'expert'))
Inputs may be any that keep to these rules, and one draw needn't show every extreme that they name: `routes`: in each step, the 16 rows of one aligned block name each expert at most 2 times, and some block names some expert exactly 2 times. `page_counts`: each block's counts sum to 32, and the largest count of a block is exactly 10. Each row of page_order is a permutation of 0 to 31.
All inputs are finite; a program needn't handle non-finite values.
Results may differ from a plain program's by a relative error of at most 0.0095.
Values may be sent and summed in bfloat16 or wider, within the bound.
No kernel may reach another device: no remote copies, remote signals or barrier semaphores. Data moves between devices by JAX's collectives and lax.ppermute only.
A program may use at most 192 MiB of HBM per device.

v0:
```python
import jax
import jax.numpy as jnp
from jax import lax
from jax.sharding import PartitionSpec as P

HEADS = 64
KV_HEADS = 8
HEAD_DIM = 64
EXPERTS = 64
MOST = 2
STEPS = 2
BLOCK = 16


def page_layout(counts, page_perm, most_pages):
    starts = jnp.cumsum(counts) - counts
    offsets = jnp.arange(most_pages, dtype=jnp.int32)
    places = starts[:, None] + offsets[None, :]
    places = jnp.where(offsets[None, :] < counts[:, None], places, 0)
    return jnp.take(page_perm, places, axis=0)


def attention(query_rows, fresh_keys, fresh_values, space_keys, space_values, counts, page_perm):
    group_size = HEADS // KV_HEADS
    most_pages = page_perm.shape[0] // 3
    row_count = counts.shape[0]
    cache_span = most_pages * BLOCK
    slot_ids = page_layout(counts, page_perm, most_pages).reshape(-1)
    cache_keys = jnp.take(space_keys, slot_ids, axis=0).reshape(
        row_count, cache_span, KV_HEADS, HEAD_DIM
    )
    cache_values = jnp.take(space_values, slot_ids, axis=0).reshape(
        row_count, cache_span, KV_HEADS, HEAD_DIM
    )
    live_mask = jnp.arange(cache_span)[None, :] < (counts * BLOCK)[:, None]
    query_heads = query_rows.reshape(STEPS, row_count, KV_HEADS, group_size, HEAD_DIM)
    new_keys = fresh_keys.reshape(STEPS, row_count, KV_HEADS, HEAD_DIM)
    new_values = fresh_values.reshape(STEPS, row_count, KV_HEADS, HEAD_DIM)
    score_scale = HEAD_DIM ** (-0.5)
    old_scores = (
        jnp.einsum("trkgh,rlkh->trkgl", query_heads, cache_keys, preferred_element_type=jnp.float32)
        * score_scale
    )
    old_scores = jnp.where(live_mask[None, :, None, None, :], old_scores, -jnp.inf)
    new_scores = (
        jnp.einsum("trkgh,urkh->trkgu", query_heads, new_keys, preferred_element_type=jnp.float32)
        * score_scale
    )
    causal = jnp.arange(STEPS)[None, :] <= jnp.arange(STEPS)[:, None]
    new_scores = jnp.where(causal[:, None, None, None, :], new_scores, -jnp.inf)
    row_max = jnp.maximum(jnp.max(old_scores, axis=-1), jnp.max(new_scores, axis=-1))
    old_probs = jnp.exp(old_scores - row_max[..., None])
    new_probs = jnp.exp(new_scores - row_max[..., None])
    denominator = jnp.sum(old_probs, axis=-1) + jnp.sum(new_probs, axis=-1)
    numerator = jnp.einsum(
        "trkgl,rlkh->trkgh",
        old_probs.astype(jnp.bfloat16),
        cache_values,
        preferred_element_type=jnp.float32,
    )
    numerator = numerator + jnp.einsum(
        "trkgu,urkh->trkgh",
        new_probs.astype(jnp.bfloat16),
        new_values,
        preferred_element_type=jnp.float32,
    )
    result = numerator / denominator[..., None]
    return result.reshape(STEPS, row_count, HEADS * HEAD_DIM).astype(jnp.bfloat16)


def route_tables(expert_ids, gate_vals):
    numbers = jnp.arange(EXPERTS, dtype=jnp.int32)
    picked = (expert_ids[..., None] == numbers).astype(jnp.int32)
    per_row = jnp.sum(picked, axis=2)
    earlier = jnp.cumsum(per_row, axis=1) - per_row
    rank_vals = jnp.sum(picked * earlier[:, :, None, :], axis=3)
    targets = expert_ids * MOST + rank_vals
    places = jnp.arange(EXPERTS * MOST, dtype=jnp.int32)
    matches = targets[..., None] == places
    sender = jnp.any(matches, axis=2).astype(jnp.bfloat16)
    weights = jnp.sum(
        jnp.where(matches, gate_vals[..., None].astype(jnp.float32), 0.0), axis=2
    ).astype(jnp.bfloat16)
    return (sender, weights)


def expert_block(slot_rows, w_gate, w_up, w_down):
    gate_part = jnp.einsum(
        "pkxmd,xdf->pkxmf", slot_rows, w_gate, preferred_element_type=jnp.float32
    )
    up_part = jnp.einsum("pkxmd,xdf->pkxmf", slot_rows, w_up, preferred_element_type=jnp.float32)
    hidden_act = ((up_part + 1.0) * gate_part * jax.nn.sigmoid(1.702 * gate_part)).astype(
        jnp.bfloat16
    )
    return jnp.einsum(
        "pkxmf,xfd->pkxmd", hidden_act, w_down, preferred_element_type=jnp.float32
    ).astype(jnp.bfloat16)


def moe_step(hidden_rows, norm_gain, router, expert_ids, w_gate, w_up, w_down):
    residual = hidden_rows.astype(jnp.float32)
    scale_rows = lax.rsqrt(jnp.mean(residual * residual, axis=1, keepdims=True) + 1e-05)
    normed = (residual * scale_rows * norm_gain).astype(jnp.bfloat16)
    logit_rows = jnp.dot(normed, router, preferred_element_type=jnp.float32)
    numbers = jnp.arange(EXPERTS, dtype=jnp.int32)
    chosen = jnp.sum(
        jnp.where(expert_ids[..., None] == numbers, logit_rows[:, None, :], 0.0), axis=-1
    )
    spreads = chosen[:, None, :] - chosen[:, :, None]
    gate_vals = (1.0 / jnp.sum(jnp.exp(spreads), axis=2)).astype(jnp.bfloat16)
    model_width = residual.shape[1]
    columns = lax.axis_size("expert")
    local_experts = w_gate.shape[0]
    group_rows, group_ids, group_gates = (
        lax.all_gather(normed[None], "dp", axis=0, tiled=True),
        lax.all_gather(expert_ids.astype(jnp.bfloat16)[None], "dp", axis=0, tiled=True),
        lax.all_gather(gate_vals[None], "dp", axis=0, tiled=True),
    )
    sender, weights = route_tables(group_ids.astype(jnp.int32), group_gates)
    packed = jnp.einsum(
        "prs,prd->psd", sender, group_rows, preferred_element_type=jnp.float32
    ).astype(jnp.bfloat16)
    packed = packed.reshape(packed.shape[0], columns, local_experts, MOST, model_width)
    partial_out = expert_block(
        lax.all_to_all(packed, "expert", split_axis=1, concat_axis=1, tiled=True),
        w_gate,
        w_up,
        w_down,
    )
    returned = lax.all_to_all(partial_out, "expert", split_axis=1, concat_axis=1, tiled=True)
    returned = returned.reshape(returned.shape[0], EXPERTS * MOST, model_width)
    row_terms = jnp.einsum("prs,psd->prd", weights, returned, preferred_element_type=jnp.float32)
    branch_out = lax.psum_scatter(row_terms, "dp", scatter_dimension=0, tiled=True)[0]
    return (residual + branch_out).astype(jnp.bfloat16)


def body(
    hidden,
    norm_gain,
    router,
    routes,
    w_gate,
    w_up,
    w_down,
    queries,
    new_key,
    new_value,
    key_pages,
    value_pages,
    page_counts,
    page_order,
):
    host_keys, host_values = (
        lax.all_to_all(key_pages, "dp", split_axis=0, concat_axis=0, tiled=True),
        lax.all_to_all(value_pages, "dp", split_axis=0, concat_axis=0, tiled=True),
    )
    kv_width = KV_HEADS * HEAD_DIM
    space_keys = host_keys.reshape(-1, BLOCK, kv_width)
    space_values = host_values.reshape(-1, BLOCK, kv_width)
    context = attention(
        queries, new_key, new_value, space_keys, space_values, page_counts[0], page_order[0]
    )
    outputs = []
    for step_index in range(STEPS):
        outputs.append(
            moe_step(
                hidden[step_index], norm_gain, router, routes[step_index], w_gate, w_up, w_down
            )
        )
    return (context, jnp.stack(outputs))


def solution(mesh):
    return jax.shard_map(
        body,
        mesh=mesh,
        in_specs=(
            P(None, ("dp", "expert"), None),
            P(),
            P(),
            P(None, ("dp", "expert"), None),
            P("expert", None, "dp"),
            P("expert", None, "dp"),
            P("expert", "dp", None),
            P(None, ("dp", "expert"), None),
            P(None, ("dp", "expert"), None),
            P(None, ("dp", "expert"), None),
            P(("dp", "expert"), None, None, None),
            P(("dp", "expert"), None, None, None),
            P(("dp", "expert"), None),
            P(("dp", "expert"), None),
        ),
        out_specs=(P(None, ("dp", "expert"), None), P(None, ("dp", "expert"), None)),
        check_vma=False,
    )
```

profile of v0, /device:TPU:0, one launch (start us, length us, event | category | flops | bytes accessed | tf_op | source)
XLA Modules:
  0.0 657.7 jit_solution(8892093810396671834)
XLA Ops:
  7.2 5.3 all-to-all-start
  12.5 0.7 slice_bitcast_fusion.1
  13.2 12.1 %all_gather.18 = bf16[8,16,4]{1,2,0:T(4,128)(2,1)S(1)} all-gather(bf16[1,16,4]{1,2,0:T(4,128)(2,1)S(1)} %get-tuple-element.14), channel_id=1, replica_groups=mesh['dp'=8,'expert'=4] {'dp'}, dimensions={0}, use_global_device_ids=true | all-gather | bytes 1152 | tf_op jit(solution)/shard_map/all_gather | solution.py:116
  25.5 1.1 fusion.105
  26.6 1.1 fusion.109
  27.7 0.7 select_reduce_fusion.3
  28.4 9.4 %all_gather.20 = bf16[8,16,2880]{2,1,0:T(8,128)(2,1)S(1)} all-gather(bf16[1,16,2880]{2,1,0:T(8,128)(2,1)S(1)} %get-tuple-element.7), channel_id=1, replica_groups=mesh['dp'=8,'expert'=4] {'dp'}, dimensions={0}, use_global_device_ids=true | all-gather | bytes 829440 | tf_op jit(solution)/shard_map/all_gather | solution.py:115
  37.8 3.5 all-to-all-start.1
  41.5 4.0 convolution_convert_fusion.1
  45.5 8.8 %copy.98 = bf16[8,128,2880]{2,0,1:T(8,128)(2,1)} copy(bf16[8,128,2880]{1,2,0:T(8,128)(2,1)} %convolution_convert_fusion.1) | data formatting | bytes 11796480 | tf_op jit(solution)/shard_map/convert_element_type | solution.py:122
  54.3 5.2 all-to-all-start.2
  59.5 9.3 %all_gather.21 = bf16[8,16,4]{1,2,0:T(4,128)(2,1)S(1)} all-gather(bf16[1,16,4]{1,2,0:T(4,128)(2,1)S(1)} %get-tuple-element.13), channel_id=1, replica_groups=mesh['dp'=8,'expert'=4] {'dp'}, dimensions={0}, use_global_device_ids=true | all-gather | bytes 1152 | tf_op jit(solution)/shard_map/all_gather | solution.py:116
  69.0 0.7 select_reduce_fusion.1
  69.9 10.4 %all_gather.23 = bf16[8,16,2880]{2,1,0:T(8,128)(2,1)S(1)} all-gather(bf16[1,16,2880]{2,1,0:T(8,128)(2,1)S(1)} %get-tuple-element.8), channel_id=1, replica_groups=mesh['dp'=8,'expert'=4] {'dp'}, dimensions={0}, use_global_device_ids=true | all-gather | bytes 829440 | tf_op jit(solution)/shard_map/all_gather | solution.py:115
  80.3 4.0 convolution_convert_fusion
  84.2 8.8 %copy.106 = bf16[8,128,2880]{2,0,1:T(8,128)(2,1)} copy(bf16[8,128,2880]{1,2,0:T(8,128)(2,1)} %convolution_convert_fusion) | data formatting | bytes 11796480 | tf_op jit(solution)/shard_map/convert_element_type | solution.py:122
  93.1 99.8 %all-to-all-done.2 = bf16[8,4,16,2,2880]{4,0,3,2,1:T(8,128)(2,1)} async-done(((bf16[8,4,16,2,2880]{4,0,3,2,1:T(8,128)(2,1)}), bf16[8,4,16,2,2880]{4,0,3,2,1:T(8,128)(2,1)}, u32[]{:S(2)}, u32[]{:S(2)}) %all-to-all-start.2) | async-done | bytes 5898272 | tf_op jit(solution)/shard_map/all_to_all | solution.py:125
  192.9 5.5 all-to-all-start.4
  198.4 13.3 %fusion.6 = f32[16,8,4,2,256]{4,1,3,2,0:T(8,128)S(1)} fusion(bf16[16,2880,256]{2,1,0:T(8,128)(2,1)} %param.20, bf16[8,4,16,2,2880]{4,0,3,2,1:T(8,128)(2,1)} %all-to-all-done.2), kind=kOutput, calls=%fused_computation.9 | convolution fusion | flops 1509949440 | bytes 30539776 | tf_op jit(solution)/shard_map/pkxmd,xdf->pkxmf/dot_general | solution.py:88
  211.7 13.3 %fusion.77 = bf16[8,4,16,2,256]{4,0,3,1,2:T(8,128)(2,1)S(1)} fusion(f32[16,8,4,2,256]{4,1,3,2,0:T(8,128)S(1)} %fusion.6, bf16[16,2880,256]{2,1,0:T(8,128)(2,1)} %param.21, bf16[8,4,16,2,2880]{4,0,3,2,1:T(8,128)(2,1)} %all-to-all-done.2), kind=kOutput, calls=%fused_computation.52 | convolution fusion | flops 1512046592 | bytes 31064064 | tf_op jit(solution)/shard_map/pkxmd,xdf->pkxmf/dot_general | solution.py:91
  225.0 12.9 %convert_bitcast_fusion.1 = bf16[8,4,16,2,2880]{4,0,3,1,2:T(8,128)(2,1)} fusion(bf16[8,4,16,2,256]{4,0,3,1,2:T(8,128)(2,1)S(1)} %fusion.77, bf16[16,256,2880]{1,2,0:T(8,128)(2,1)} %param.22), kind=kOutput, calls=%fused_computation.20 | convolution fusion | flops 1512898560 | bytes 30015488 | tf_op jit(solution)/shard_map/pkxmf,xfd->pkxmd/dot_general | solution.py:95
  237.8 5.7 copy.101
  243.6 87.4 %all-to-all-done.4 = bf16[8,4,16,2,2880]{4,0,3,2,1:T(8,128)(2,1)} async-done(((bf16[8,4,16,2,2880]{4,0,3,2,1:T(8,128)(2,1)}), bf16[8,4,16,2,2880]{4,0,3,2,1:T(8,128)(2,1)}, u32[]{:S(2)}, u32[]{:S(2)}) %all-to-all-start.4) | async-done | bytes 5898272 | tf_op jit(solution)/shard_map/all_to_all | solution.py:125
  331.0 5.8 all-to-all-start.3
  336.8 13.3 %fusion.4 = f32[16,8,4,2,256]{4,1,3,2,0:T(8,128)S(1)} fusion(bf16[16,2880,256]{2,1,0:T(8,128)(2,1)} %param.20, bf16[8,4,16,2,2880]{4,0,3,2,1:T(8,128)(2,1)} %all-to-all-done.4), kind=kOutput, calls=%fused_computation.7 | convolution fusion | flops 1509949440 | bytes 30539776 | tf_op jit(solution)/shard_map/pkxmd,xdf->pkxmf/dot_general | solution.py:88
  350.1 13.3 %fusion.82 = bf16[8,4,16,2,256]{4,0,3,1,2:T(8,128)(2,1)S(1)} fusion(f32[16,8,4,2,256]{4,1,3,2,0:T(8,128)S(1)} %fusion.4, bf16[16,2880,256]{2,1,0:T(8,128)(2,1)} %param.21, bf16[8,4,16,2,2880]{4,0,3,2,1:T(8,128)(2,1)} %all-to-all-done.4), kind=kOutput, calls=%fused_computation.53 | convolution fusion | flops 1512046592 | bytes 31064064 | tf_op jit(solution)/shard_map/pkxmd,xdf->pkxmf/dot_general | solution.py:91
  363.3 12.9 %convert_bitcast_fusion = bf16[8,4,16,2,2880]{4,0,3,1,2:T(8,128)(2,1)} fusion(bf16[8,4,16,2,256]{4,0,3,1,2:T(8,128)(2,1)S(1)} %fusion.82, bf16[16,256,2880]{1,2,0:T(8,128)(2,1)} %param.22), kind=kOutput, calls=%fused_computation.19 | convolution fusion | flops 1512898560 | bytes 30015488 | tf_op jit(solution)/shard_map/pkxmf,xfd->pkxmd/dot_general | solution.py:95
  376.2 5.7 copy.109
  381.9 86.9 %all-to-all-done.3 = bf16[8,4,16,2,2880]{4,0,3,2,1:T(8,128)(2,1)} async-done(((bf16[8,4,16,2,2880]{4,0,3,2,1:T(8,128)(2,1)}), bf16[8,4,16,2,2880]{4,0,3,2,1:T(8,128)(2,1)}, u32[]{:S(2)}, u32[]{:S(2)}) %all-to-all-start.3) | async-done | bytes 5898272 | tf_op jit(solution)/shard_map/all_to_all | solution.py:130
  468.8 5.2 all-to-all-start.5
  474.9 8.7 %all-gather.2 = bf16[8,16,4]{1,2,0:T(4,128)(2,1)S(1)} all-gather(bf16[1,16,4]{1,2,0:T(4,128)(2,1)S(1)} %fusion.134), channel_id=2, replica_groups=mesh['dp'=8,'expert'=4] {'dp'}, dimensions={0}, use_global_device_ids=true | all-gather | bytes 1152 | tf_op jit(solution)/shard_map/all_gather | solution.py:117
  483.9 5.5 fusion.14
  489.5 9.0 %all-gather.3 = bf16[8,16,4]{1,2,0:T(4,128)(2,1)S(1)} all-gather(bf16[1,16,4]{1,2,0:T(4,128)(2,1)S(1)} %fusion.135), channel_id=3, replica_groups=mesh['dp'=8,'expert'=4] {'dp'}, dimensions={0}, use_global_device_ids=true | all-gather | bytes 1152 | tf_op jit(solution)/shard_map/all_gather | solution.py:117
  500.2 1.6 gather_fusion
  502.1 3.1 fusion.138
  505.2 2.5 gather_fusion.1
  507.6 2.5 gather_fusion.2
  510.1 95.9 %all-to-all-done.5 = bf16[8,4,16,2,2880]{4,0,3,2,1:T(8,128)(2,1)} async-done(((bf16[8,4,16,2,2880]{4,0,3,2,1:T(8,128)(2,1)}), bf16[8,4,16,2,2880]{4,0,3,2,1:T(8,128)(2,1)}, u32[]{:S(2)}, u32[]{:S(2)}) %all-to-all-start.5) | async-done | bytes 5898272 | tf_op jit(solution)/shard_map/all_to_all | solution.py:130
  606.0 5.5 fusion.12
  611.6 4.1 broadcast_select_fusion
  615.7 7.7 %reshape.331 = bf16[16,160,8,64]{3,2,1,0:T(8,128)(2,1)} reshape(bf16[160,16,512]{2,1,0:T(8,128)(2,1)} %get-tuple-element.17) | data formatting | bytes 5242880 | tf_op jit(solution)/shard_map/reshape | solution.py:29
  623.4 4.8 reshape.329
  628.2 5.7 bitcast_reduce_fusion
  634.5 1.0 fusion.29
  635.6 1.5 fusion.31
  637.9 1.2 convert_element_type.141
  639.1 9.8 %reduce-scatter.5.cloned.1.call-done = f32[1,16,2880]{2,1,0:T(8,128)} async-done(((f32[8,16,2880]{2,1,0:T(8,128)}), f32[1,16,2880]{2,1,0:T(8,128)}) %reduce-scatter.5.cloned.1.call-update) | async-done | bytes 184336 | tf_op jit(solution)/shard_map/reduce_scatter | solution.py:133
  648.8 1.0 fusion.110
  (84 shorter events, 5.8 us)
Async XLA Ops:
  7.2 467.0 %copy-start = (bf16[2880,64]{0,1:T(8,128)(2,1)S(1)}, bf16[2880,64]{0,1:T(8,128)(2,1)}, u32[]{:S(2)}) copy-start(bf16[2880,64]{0,1:T(8,128)(2,1)} %param.18) | copy-start | bytes 1105924
  7.2 30.6 %all-to-all-start = ((bf16[8,4,16,512]{3,2,1,0:T(8,128)(2,1)}), bf16[8,4,16,512]{3,2,1,0:T(8,128)(2,1)S(1)}, u32[]{:S(2)}, u32[]{:S(2)}) async-start(bf16[8,4,16,512]{3,2,1,0:T(8,128)(2,1)} %param.27), calls=%async_computation | async-start | bytes 1048576 | tf_op jit(solution)/shard_map/all_to_all | solution.py:155
  37.8 16.4 %all-to-all-start.1 = ((bf16[8,4,16,512]{3,2,1,0:T(8,128)(2,1)}), bf16[8,4,16,512]{3,2,1,0:T(8,128)(2,1)S(1)}, u32[]{:S(2)}, u32[]{:S(2)}) async-start(bf16[8,4,16,512]{3,2,1,0:T(8,128)(2,1)} %param.26), calls=%async_computation.1 | async-start | bytes 1048576 | tf_op jit(solution)/shard_map/all_to_all | solution.py:154
  54.3 138.6 %all-to-all-start.2 = ((bf16[8,4,16,2,2880]{4,0,3,2,1:T(8,128)(2,1)}), bf16[8,4,16,2,2880]{4,0,3,2,1:T(8,128)(2,1)}, u32[]{:S(2)}, u32[]{:S(2)}) async-start(bf16[8,4,16,2,2880]{4,0,3,2,1:T(8,128)(2,1)} %bitcast.145), calls=%async_computation.2 | async-start | bytes 12058624 | tf_op jit(solution)/shard_map/all_to_all | solution.py:125
  192.9 138.1 %all-to-all-start.4 = ((bf16[8,4,16,2,2880]{4,0,3,2,1:T(8,128)(2,1)}), bf16[8,4,16,2,2880]{4,0,3,2,1:T(8,128)(2,1)}, u32[]{:S(2)}, u32[]{:S(2)}) async-start(bf16[8,4,16,2,2880]{4,0,3,2,1:T(8,128)(2,1)} %bitcast.146), calls=%async_computation.5 | async-start | bytes 12058624 | tf_op jit(solution)/shard_map/all_to_all | solution.py:125
  331.0 137.8 %all-to-all-start.3 = ((bf16[8,4,16,2,2880]{4,0,3,2,1:T(8,128)(2,1)}), bf16[8,4,16,2,2880]{4,0,3,2,1:T(8,128)(2,1)}, u32[]{:S(2)}, u32[]{:S(2)}) async-start(bf16[8,4,16,2,2880]{4,0,3,2,1:T(8,128)(2,1)} %copy.101), calls=%async_computation.3 | async-start | bytes 12058624 | tf_op jit(solution)/shard_map/all_to_all | solution.py:130
  381.9 92.2 %copy-start.5 = (bf16[2,16,2880]{2,1,0:T(8,128)(2,1)S(1)}, bf16[2,16,2880]{2,1,0:T(8,128)(2,1)}, u32[]{:S(2)}) copy-start(bf16[2,16,2880]{2,1,0:T(8,128)(2,1)} %param.16) | copy-start | bytes 552964
  381.9 92.2 %copy-start.9 = (f32[2880]{0:T(1024)S(1)}, f32[2880]{0:T(1024)}, u32[]{:S(2)}) copy-start(f32[2880]{0:T(1024)} %param.17) | copy-start | bytes 34564
  468.8 137.2 %all-to-all-start.5 = ((bf16[8,4,16,2,2880]{4,0,3,2,1:T(8,128)(2,1)}), bf16[8,4,16,2,2880]{4,0,3,2,1:T(8,128)(2,1)}, u32[]{:S(2)}, u32[]{:S(2)}) async-start(bf16[8,4,16,2,2880]{4,0,3,2,1:T(8,128)(2,1)} %copy.109), calls=%async_computation.6 | async-start | bytes 12058624 | tf_op jit(solution)/shard_map/all_to_all | solution.py:130
  474.0 24.5 %copy-start.12 = (s32[1,16]{1,0:T(1,128)S(1)}, s32[1,16]{1,0:T(1,128)}, u32[]{:S(2)}) copy-start(s32[1,16]{1,0:T(1,128)} %param.28) | copy-start | bytes 196
  474.0 25.3 %copy-start.7 = (bf16[2,16,4096]{2,1,0:T(8,128)(2,1)S(1)}, bf16[2,16,4096]{2,1,0:T(8,128)(2,1)}, u32[]{:S(2)}) copy-start(bf16[2,16,4096]{2,1,0:T(8,128)(2,1)} %param.23) | copy-start | bytes 786436
  474.0 25.9 %copy-start.10 = (bf16[2,16,512]{2,1,0:T(8,128)(2,1)S(1)}, bf16[2,16,512]{2,1,0:T(8,128)(2,1)}, u32[]{:S(2)}) copy-start(bf16[2,16,512]{2,1,0:T(8,128)(2,1)} %param.24) | copy-start | bytes 98308
  474.1 26.0 %copy-start.11 = (bf16[2,16,512]{2,1,0:T(8,128)(2,1)S(1)}, bf16[2,16,512]{2,1,0:T(8,128)(2,1)}, u32[]{:S(2)}) copy-start(bf16[2,16,512]{2,1,0:T(8,128)(2,1)} %param.25) | copy-start | bytes 98308
  474.1 26.1 %copy-start.1 = (s32[1,32]{1,0:T(1,128)S(1)}, s32[1,32]{1,0:T(1,128)}, u32[]{:S(2)}) copy-start(s32[1,32]{1,0:T(1,128)} %param.29) | copy-start | bytes 388
  474.1 165.0 %reduce-scatter.3.cloned.1.call-start = ((), (), s32[]{:S(2)}) async-start(), calls=%async_computation.8 | async-start | bytes 1695744 | tf_op jit(solution)/shard_map/reduce_scatter | solution.py:133
  489.4 159.4 %reduce-scatter.5.cloned.1.call-start = ((), (), s32[]{:S(2)}) async-start(), calls=%async_computation.9 | async-start | bytes 1695744 | tf_op jit(solution)/shard_map/reduce_scatter | solution.py:133
  499.9 7.7 %copy-start.6 = (bf16[2,16,8,8,64]{4,3,2,1,0:T(8,128)(2,1)}, bf16[2,16,8,8,64]{4,3,2,1,0:T(8,128)(2,1)S(1)}, u32[]{:S(2)}) copy-start(bf16[2,16,8,8,64]{4,3,2,1,0:T(8,128)(2,1)S(1)} %reshape.332) | copy-start | bytes 786436
  510.1 101.4 %copy-start.2 = (bf16[160,16,512]{2,1,0:T(8,128)(2,1)S(1)}, bf16[160,16,512]{2,1,0:T(8,128)(2,1)}, u32[]{:S(2)}) copy-start(bf16[160,16,512]{2,1,0:T(8,128)(2,1)} %gather_fusion.1) | copy-start | bytes 7864324
  615.7 7.7 %copy-start.3 = (bf16[160,16,512]{2,1,0:T(8,128)(2,1)S(1)}, bf16[160,16,512]{2,1,0:T(8,128)(2,1)}, u32[]{:S(2)}) copy-start(bf16[160,16,512]{2,1,0:T(8,128)(2,1)} %get-tuple-element.18) | copy-start | bytes 7864324
  628.2 5.8 copy-start.8
  628.2 7.4 %copy-start.4 = (bf16[16,160,8,64]{3,2,1,0:T(8,128)(2,1)S(1)}, bf16[16,160,8,64]{3,2,1,0:T(8,128)(2,1)}, u32[]{:S(2)}) copy-start(bf16[16,160,8,64]{3,2,1,0:T(8,128)(2,1)} %reshape.329) | copy-start | bytes 7864324
Sparse Core Ops, SparseCore 0:
  489.5 38.6 reduce-scatter.2
  611.7 37.1 reduce-scatter.4
where the time goes:
time: 665 us; the launch traced here: 658 us
  waiting for transfers between devices  380 us (57%)
  matrix products  109 us (16%)
  blocking collectives  58.9 us (9%)
  local copies, waits for them, and re-layouts  50.8 us (8%)
  starting transfers between devices  30.6 us (5%)
  between operations  14.8 us (2%)
  other arithmetic  13.5 us (2%)
    all_to_all x2, waiting for transfers between devices, moe_step(): lax.all_to_all(packed, 'expert', split_axis=1, concat_axis=1, tiled=True)  187 us
    all_to_all x2, waiting for transfers between devices, moe_step(): lax.all_to_all(partial_out, 'expert', split_axis=1, concat_axis=1, tiled=...  183 us
    dot_general x2, matrix products, expert_block(): jnp.einsum('pkxmd,xdf->pkxmf', slot_rows, w_gate, preferred_element_type=...  26.6 us
    dot_general x2, matrix products, expert_block(): jnp.einsum('pkxmd,xdf->pkxmf', slot_rows, w_up, preferred_element_type=jn...  26.5 us
    dot_general x2, matrix products, expert_block(): jnp.einsum('pkxmf,xfd->pkxmd', hidden_act, w_down, preferred_element_type...  25.7 us
    all_gather x2, blocking collectives, moe_step(): lax.all_gather(expert_ids.astype(jnp.bfloat16)[None], 'dp', axis=0, tiled...  21.4 us
    all_gather x2, blocking collectives, moe_step(): lax.all_gather(normed[None], 'dp', axis=0, tiled=True)  19.7 us
    all_gather x2, blocking collectives, moe_step(): lax.all_gather(gate_vals[None], 'dp', axis=0, tiled=True)  17.7 us
  transfers between devices with their start and end apart: 8, of which 5 were waited for; matrix products, arithmetic and copies ran while one was open for 26% of the time, Pallas kernels for 0%

commit v1 on v0

--- a/solution.py
+++ b/solution.py
@@ -127,7 +127,9 @@
         w_up,
         w_down,
     )
-    returned = lax.all_to_all(partial_out, "expert", split_axis=1, concat_axis=1, tiled=True)
+    cells = jnp.split(partial_out, lax.axis_size("expert"), axis=1)
+    incoming = lax.all_to_all(jnp.stack(cells), "expert", 0, 0)
+    returned = jnp.concatenate(incoming, axis=1)
     returned = returned.reshape(returned.shape[0], EXPERTS * MOST, model_width)
     row_terms = jnp.einsum("prs,psd->prd", weights, returned, preferred_element_type=jnp.float32)
     branch_out = lax.psum_scatter(row_terms, "dp", scatter_dimension=0, tiled=True)[0]

time: 665 us -> 664 us (level)
  other arithmetic: 13.5 us -> 22 us
    convert_element_type x2 -> x0, local copies, waits for them, and re-layouts: 11.4 us -> none  [expert_block(): return jnp.einsum('pkxmf,xfd->pkxmd', hidden_act, w_down, preferred_eleme...]
    another operation x2 -> x4, other arithmetic: 0.16 us -> 8.59 us  [the longest x2 8.44 us: moe_step(): incoming = lax.all_to_all(jnp.stack(cells), 'expert', 0, 0)]
  transfers between devices with their start and end apart: 8 -> 8, of which waited for: 5 -> 5; matrix products, arithmetic and copies ran while one was open for 26% -> 27% of each run, Pallas kernels for 0% -> 0%
where the time goes in v1:
time: 664 us; the launch traced here: 658 us
  waiting for transfers between devices  376 us (57%)
  matrix products  109 us (16%)
  blocking collectives  58.9 us (9%)
  local copies, waits for them, and re-layouts  45.8 us (7%)
  starting transfers between devices  30.5 us (5%)
  other arithmetic  22 us (3%)
  between operations  14.8 us (2%)
    all_to_all x2, waiting for transfers between devices, moe_step(): lax.all_to_all(packed, 'expert', split_axis=1, concat_axis=1, tiled=True)  186 us
    all_to_all x2, waiting for transfers between devices, moe_step(): incoming = lax.all_to_all(jnp.stack(cells), 'expert', 0, 0)  181 us
    dot_general x2, matrix products, expert_block(): jnp.einsum('pkxmd,xdf->pkxmf', slot_rows, w_gate, preferred_element_type=...  26.6 us
    dot_general x2, matrix products, expert_block(): jnp.einsum('pkxmd,xdf->pkxmf', slot_rows, w_up, preferred_element_type=jn...  26.5 us
    dot_general x2, matrix products, expert_block(): jnp.einsum('pkxmf,xfd->pkxmd', hidden_act, w_down, preferred_element_type...  25.8 us
    all_gather x2, blocking collectives, moe_step(): lax.all_gather(expert_ids.astype(jnp.bfloat16)[None], 'dp', axis=0, tiled...  21.4 us
    all_gather x2, blocking collectives, moe_step(): lax.all_gather(normed[None], 'dp', axis=0, tiled=True)  19.7 us
    all_gather x2, blocking collectives, moe_step(): lax.all_gather(gate_vals[None], 'dp', axis=0, tiled=True)  17.8 us
  transfers between devices with their start and end apart: 8, of which 5 were waited for; matrix products, arithmetic and copies ran while one was open for 27% of the time, Pallas kernels for 0%

profile of v1, /device:TPU:0, one launch (start us, length us, event | category | flops | bytes accessed | tf_op | source)
XLA Modules:
  0.0 657.6 jit_solution(6123735257518678812)
XLA Ops:
  7.2 5.3 all-to-all-start
  13.2 12.1 %all_gather.21 = bf16[8,16,4]{1,2,0:T(4,128)(2,1)S(1)} all-gather(bf16[1,16,4]{1,2,0:T(4,128)(2,1)S(1)} %get-tuple-element.21), channel_id=1, replica_groups=mesh['dp'=8,'expert'=4] {'dp'}, dimensions={0}, use_global_device_ids=true | all-gather | bytes 1152 | tf_op jit(solution)/shard_map/all_gather | solution.py:116
  25.5 1.1 fusion.105
  26.6 1.1 fusion.109
  28.4 9.4 %all_gather.23 = bf16[8,16,2880]{2,1,0:T(8,128)(2,1)S(1)} all-gather(bf16[1,16,2880]{2,1,0:T(8,128)(2,1)S(1)} %get-tuple-element.16), channel_id=1, replica_groups=mesh['dp'=8,'expert'=4] {'dp'}, dimensions={0}, use_global_device_ids=true | all-gather | bytes 829440 | tf_op jit(solution)/shard_map/all_gather | solution.py:115
  37.8 3.5 all-to-all-start.1
  41.5 4.0 convolution_convert_fusion
  45.5 8.8 %copy.124 = bf16[8,128,2880]{2,0,1:T(8,128)(2,1)} copy(bf16[8,128,2880]{1,2,0:T(8,128)(2,1)} %convolution_convert_fusion) | data formatting | bytes 11796480 | tf_op jit(solution)/shard_map/convert_element_type | solution.py:122
  54.3 5.3 all-to-all-start.4
  59.5 9.3 %all_gather.18 = bf16[8,16,4]{1,2,0:T(4,128)(2,1)S(1)} all-gather(bf16[1,16,4]{1,2,0:T(4,128)(2,1)S(1)} %get-tuple-element.22), channel_id=1, replica_groups=mesh['dp'=8,'expert'=4] {'dp'}, dimensions={0}, use_global_device_ids=true | all-gather | bytes 1152 | tf_op jit(solution)/shard_map/all_gather | solution.py:116
  69.1 0.7 select_reduce_fusion.3
  70.0 10.4 %all_gather.20 = bf16[8,16,2880]{2,1,0:T(8,128)(2,1)S(1)} all-gather(bf16[1,16,2880]{2,1,0:T(8,128)(2,1)S(1)} %get-tuple-element.15), channel_id=1, replica_groups=mesh['dp'=8,'expert'=4] {'dp'}, dimensions={0}, use_global_device_ids=true | all-gather | bytes 829440 | tf_op jit(solution)/shard_map/all_gather | solution.py:115
  80.3 4.0 convolution_convert_fusion.1
  84.3 8.8 %copy.114 = bf16[8,128,2880]{2,0,1:T(8,128)(2,1)} copy(bf16[8,128,2880]{1,2,0:T(8,128)(2,1)} %convolution_convert_fusion.1) | data formatting | bytes 11796480 | tf_op jit(solution)/shard_map/convert_element_type | solution.py:122
  93.1 99.8 %all-to-all-done.4 = bf16[8,4,16,2,2880]{4,0,3,2,1:T(8,128)(2,1)} async-done(((bf16[8,4,16,2,2880]{4,0,3,2,1:T(8,128)(2,1)}), bf16[8,4,16,2,2880]{4,0,3,2,1:T(8,128)(2,1)}, u32[]{:S(2)}, u32[]{:S(2)}) %all-to-all-start.4) | async-done | bytes 5898272 | tf_op jit(solution)/shard_map/all_to_all | solution.py:125
  192.9 5.7 all-to-all-start.2
  198.7 13.3 %fusion.4 = f32[16,8,4,2,256]{4,1,3,2,0:T(8,128)S(1)} fusion(bf16[16,2880,256]{2,1,0:T(8,128)(2,1)} %param.20, bf16[8,4,16,2,2880]{4,0,3,2,1:T(8,128)(2,1)} %all-to-all-done.4), kind=kOutput, calls=%fused_computation.7 | convolution fusion | flops 1509949440 | bytes 30539776 | tf_op jit(solution)/shard_map/pkxmd,xdf->pkxmf/dot_general | solution.py:88
  212.0 13.3 %fusion.82 = bf16[8,4,16,2,256]{4,0,3,1,2:T(8,128)(2,1)S(1)} fusion(f32[16,8,4,2,256]{4,1,3,2,0:T(8,128)S(1)} %fusion.4, bf16[16,2880,256]{2,1,0:T(8,128)(2,1)} %param.21, bf16[8,4,16,2,2880]{4,0,3,2,1:T(8,128)(2,1)} %all-to-all-done.4), kind=kOutput, calls=%fused_computation.63 | convolution fusion | flops 1512046592 | bytes 31064064 | tf_op jit(solution)/shard_map/pkxmd,xdf->pkxmf/dot_general | solution.py:91
  225.2 12.9 %convert_bitcast_fusion = bf16[8,4,16,2,2880]{4,0,3,1,2:T(8,128)(2,1)} fusion(bf16[8,4,16,2,256]{4,0,3,1,2:T(8,128)(2,1)S(1)} %fusion.82, bf16[16,256,2880]{1,2,0:T(8,128)(2,1)} %param.22), kind=kOutput, calls=%fused_computation.21 | convolution fusion | flops 1512898560 | bytes 30015488 | tf_op jit(solution)/shard_map/pkxmf,xfd->pkxmd/dot_general | solution.py:95
  238.1 3.2 slice_bitcast_fusion.3
  241.3 4.2 pad_maximum_fusion.1
  245.4 85.8 %all-to-all-done.2 = bf16[8,4,16,2,2880]{4,0,3,2,1:T(8,128)(2,1)} async-done(((bf16[8,4,16,2,2880]{4,0,3,2,1:T(8,128)(2,1)}), bf16[8,4,16,2,2880]{4,0,3,2,1:T(8,128)(2,1)}, u32[]{:S(2)}, u32[]{:S(2)}) %all-to-all-start.2) | async-done | bytes 5898272 | tf_op jit(solution)/shard_map/all_to_all | solution.py:125
  331.3 5.4 all-to-all-start.5
  336.7 13.3 %fusion.6 = f32[16,8,4,2,256]{4,1,3,2,0:T(8,128)S(1)} fusion(bf16[16,2880,256]{2,1,0:T(8,128)(2,1)} %param.20, bf16[8,4,16,2,2880]{4,0,3,2,1:T(8,128)(2,1)} %all-to-all-done.2), kind=kOutput, calls=%fused_computation.9 | convolution fusion | flops 1509949440 | bytes 30539776 | tf_op jit(solution)/shard_map/pkxmd,xdf->pkxmf/dot_general | solution.py:88
  350.0 13.3 %fusion.77 = bf16[8,4,16,2,256]{4,0,3,1,2:T(8,128)(2,1)S(1)} fusion(f32[16,8,4,2,256]{4,1,3,2,0:T(8,128)S(1)} %fusion.6, bf16[16,2880,256]{2,1,0:T(8,128)(2,1)} %param.21, bf16[8,4,16,2,2880]{4,0,3,2,1:T(8,128)(2,1)} %all-to-all-done.2), kind=kOutput, calls=%fused_computation.62 | convolution fusion | flops 1512046592 | bytes 31064064 | tf_op jit(solution)/shard_map/pkxmd,xdf->pkxmf/dot_general | solution.py:91
  363.3 12.9 %convert_bitcast_fusion.1 = bf16[8,4,16,2,2880]{4,0,3,1,2:T(8,128)(2,1)} fusion(bf16[8,4,16,2,256]{4,0,3,1,2:T(8,128)(2,1)S(1)} %fusion.77, bf16[16,256,2880]{1,2,0:T(8,128)(2,1)} %param.22), kind=kOutput, calls=%fused_computation.22 | convolution fusion | flops 1512898560 | bytes 30015488 | tf_op jit(solution)/shard_map/pkxmf,xfd->pkxmd/dot_general | solution.py:95
  376.2 3.2 slice_bitcast_fusion.7
  379.4 4.3 pad_maximum_fusion
  383.6 85.1 %all-to-all-done.5 = bf16[4,8,1,16,2,2880]{5,1,4,3,2,0:T(8,128)(2,1)} async-done(((bf16[4,8,1,16,2,2880]{5,1,4,3,2,0:T(8,128)(2,1)}), bf16[4,8,1,16,2,2880]{5,1,4,3,2,0:T(8,128)(2,1)}, u32[]{:S(2)}, u32[]{:S(2)}) %all-to-all-start.5) | async-done | bytes 5898272 | tf_op jit(solution)/shard_map/all_to_all | solution.py:131
  468.7 5.2 all-to-all-start.3
  474.8 8.9 %all-gather.3 = bf16[8,16,4]{1,2,0:T(4,128)(2,1)S(1)} all-gather(bf16[1,16,4]{1,2,0:T(4,128)(2,1)S(1)} %fusion.135), channel_id=3, replica_groups=mesh['dp'=8,'expert'=4] {'dp'}, dimensions={0}, use_global_device_ids=true | all-gather | bytes 1152 | tf_op jit(solution)/shard_map/all_gather | solution.py:117
  484.0 5.5 fusion.12
  489.6 8.9 %all-gather.2 = bf16[8,16,4]{1,2,0:T(4,128)(2,1)S(1)} all-gather(bf16[1,16,4]{1,2,0:T(4,128)(2,1)S(1)} %fusion.134), channel_id=2, replica_groups=mesh['dp'=8,'expert'=4] {'dp'}, dimensions={0}, use_global_device_ids=true | all-gather | bytes 1152 | tf_op jit(solution)/shard_map/all_gather | solution.py:117
  500.1 1.6 gather_fusion
  502.0 3.1 fusion.138
  505.1 2.5 gather_fusion.1
  507.6 2.5 gather_fusion.2
  510.1 95.9 %all-to-all-done.3 = bf16[4,8,1,16,2,2880]{5,1,4,3,2,0:T(8,128)(2,1)} async-done(((bf16[4,8,1,16,2,2880]{5,1,4,3,2,0:T(8,128)(2,1)}), bf16[4,8,1,16,2,2880]{5,1,4,3,2,0:T(8,128)(2,1)}, u32[]{:S(2)}, u32[]{:S(2)}) %all-to-all-start.3) | async-done | bytes 5898272 | tf_op jit(solution)/shard_map/all_to_all | solution.py:131
  606.0 5.5 fusion.14
  611.5 4.1 broadcast_select_fusion
  615.6 7.7 %reshape.331 = bf16[16,160,8,64]{3,2,1,0:T(8,128)(2,1)} reshape(bf16[160,16,512]{2,1,0:T(8,128)(2,1)} %get-tuple-element.25) | data formatting | bytes 5242880 | tf_op jit(solution)/shard_map/reshape | solution.py:29
  623.3 4.8 reshape.329
  628.2 5.7 bitcast_reduce_fusion
  634.5 1.0 fusion.29
  635.6 1.5 fusion.31
  637.9 1.2 convert_element_type.141
  639.1 9.7 %reduce-scatter.3.cloned.1.call-done = f32[1,16,2880]{2,1,0:T(8,128)} async-done(((f32[8,16,2880]{2,1,0:T(8,128)}), f32[1,16,2880]{2,1,0:T(8,128)}) %reduce-scatter.3.cloned.1.call-update) | async-done | bytes 184336 | tf_op jit(solution)/shard_map/reduce_scatter | solution.py:135
  648.7 1.0 fusion.110
  (86 shorter events, 7.3 us)
Async XLA Ops:
  7.2 466.9 %copy-start = (bf16[2880,64]{0,1:T(8,128)(2,1)S(1)}, bf16[2880,64]{0,1:T(8,128)(2,1)}, u32[]{:S(2)}) copy-start(bf16[2880,64]{0,1:T(8,128)(2,1)} %param.18) | copy-start | bytes 1105924
  7.2 30.6 %all-to-all-start = ((bf16[8,4,16,512]{3,2,1,0:T(8,128)(2,1)}), bf16[8,4,16,512]{3,2,1,0:T(8,128)(2,1)S(1)}, u32[]{:S(2)}, u32[]{:S(2)}) async-start(bf16[8,4,16,512]{3,2,1,0:T(8,128)(2,1)} %param.27), calls=%async_computation | async-start | bytes 1048576 | tf_op jit(solution)/shard_map/all_to_all | solution.py:157
  37.8 16.4 %all-to-all-start.1 = ((bf16[8,4,16,512]{3,2,1,0:T(8,128)(2,1)}), bf16[8,4,16,512]{3,2,1,0:T(8,128)(2,1)S(1)}, u32[]{:S(2)}, u32[]{:S(2)}) async-start(bf16[8,4,16,512]{3,2,1,0:T(8,128)(2,1)} %param.26), calls=%async_computation.1 | async-start | bytes 1048576 | tf_op jit(solution)/shard_map/all_to_all | solution.py:156
  54.3 138.7 %all-to-all-start.4 = ((bf16[8,4,16,2,2880]{4,0,3,2,1:T(8,128)(2,1)}), bf16[8,4,16,2,2880]{4,0,3,2,1:T(8,128)(2,1)}, u32[]{:S(2)}, u32[]{:S(2)}) async-start(bf16[8,4,16,2,2880]{4,0,3,2,1:T(8,128)(2,1)} %bitcast.177), calls=%async_computation.5 | async-start | bytes 12058624 | tf_op jit(solution)/shard_map/all_to_all | solution.py:125
  192.9 138.3 %all-to-all-start.2 = ((bf16[8,4,16,2,2880]{4,0,3,2,1:T(8,128)(2,1)}), bf16[8,4,16,2,2880]{4,0,3,2,1:T(8,128)(2,1)}, u32[]{:S(2)}, u32[]{:S(2)}) async-start(bf16[8,4,16,2,2880]{4,0,3,2,1:T(8,128)(2,1)} %bitcast.178), calls=%async_computation.2 | async-start | bytes 12058624 | tf_op jit(solution)/shard_map/all_to_all | solution.py:125
  331.3 137.5 %all-to-all-start.5 = ((bf16[4,8,1,16,2,2880]{5,1,4,3,2,0:T(8,128)(2,1)}), bf16[4,8,1,16,2,2880]{5,1,4,3,2,0:T(8,128)(2,1)}, u32[]{:S(2)}, u32[]{:S(2)}) async-start(bf16[4,8,1,16,2,2880]{5,1,4,3,2,0:T(8,128)(2,1)} %pad_maximum_fusion.1), calls=%async_computation.6 | async-start | bytes 12058624 | tf_op jit(solution)/shard_map/all_to_all | solution.py:131
  383.6 90.4 %copy-start.5 = (bf16[2,16,2880]{2,1,0:T(8,128)(2,1)S(1)}, bf16[2,16,2880]{2,1,0:T(8,128)(2,1)}, u32[]{:S(2)}) copy-start(bf16[2,16,2880]{2,1,0:T(8,128)(2,1)} %param.16) | copy-start | bytes 552964
  383.6 90.4 %copy-start.9 = (f32[2880]{0:T(1024)S(1)}, f32[2880]{0:T(1024)}, u32[]{:S(2)}) copy-start(f32[2880]{0:T(1024)} %param.17) | copy-start | bytes 34564
  468.7 137.2 %all-to-all-start.3 = ((bf16[4,8,1,16,2,2880]{5,1,4,3,2,0:T(8,128)(2,1)}), bf16[4,8,1,16,2,2880]{5,1,4,3,2,0:T(8,128)(2,1)}, u32[]{:S(2)}, u32[]{:S(2)}) async-start(bf16[4,8,1,16,2,2880]{5,1,4,3,2,0:T(8,128)(2,1)} %pad_maximum_fusion), calls=%async_computation.3 | async-start | bytes 12058624 | tf_op jit(solution)/shard_map/all_to_all | solution.py:131
  474.0 24.5 %copy-start.12 = (s32[1,16]{1,0:T(1,128)S(1)}, s32[1,16]{1,0:T(1,128)}, u32[]{:S(2)}) copy-start(s32[1,16]{1,0:T(1,128)} %param.28) | copy-start | bytes 196
  474.0 25.3 %copy-start.7 = (bf16[2,16,4096]{2,1,0:T(8,128)(2,1)S(1)}, bf16[2,16,4096]{2,1,0:T(8,128)(2,1)}, u32[]{:S(2)}) copy-start(bf16[2,16,4096]{2,1,0:T(8,128)(2,1)} %param.23) | copy-start | bytes 786436
  474.0 165.1 %reduce-scatter.5.cloned.1.call-start = ((), (), s32[]{:S(2)}) async-start(), calls=%async_computation.9 | async-start | bytes 1695744 | tf_op jit(solution)/shard_map/reduce_scatter | solution.py:135
  474.3 25.6 %copy-start.10 = (bf16[2,16,512]{2,1,0:T(8,128)(2,1)S(1)}, bf16[2,16,512]{2,1,0:T(8,128)(2,1)}, u32[]{:S(2)}) copy-start(bf16[2,16,512]{2,1,0:T(8,128)(2,1)} %param.24) | copy-start | bytes 98308
  474.3 25.7 %copy-start.11 = (bf16[2,16,512]{2,1,0:T(8,128)(2,1)S(1)}, bf16[2,16,512]{2,1,0:T(8,128)(2,1)}, u32[]{:S(2)}) copy-start(bf16[2,16,512]{2,1,0:T(8,128)(2,1)} %param.25) | copy-start | bytes 98308
  474.3 25.8 %copy-start.1 = (s32[1,32]{1,0:T(1,128)S(1)}, s32[1,32]{1,0:T(1,128)}, u32[]{:S(2)}) copy-start(s32[1,32]{1,0:T(1,128)} %param.29) | copy-start | bytes 388
  489.5 159.2 %reduce-scatter.3.cloned.1.call-start = ((), (), s32[]{:S(2)}) async-start(), calls=%async_computation.8 | async-start | bytes 1695744 | tf_op jit(solution)/shard_map/reduce_scatter | solution.py:135
  499.9 7.7 %copy-start.6 = (bf16[2,16,8,8,64]{4,3,2,1,0:T(8,128)(2,1)}, bf16[2,16,8,8,64]{4,3,2,1,0:T(8,128)(2,1)S(1)}, u32[]{:S(2)}) copy-start(bf16[2,16,8,8,64]{4,3,2,1,0:T(8,128)(2,1)S(1)} %reshape.332) | copy-start | bytes 786436
  510.1 101.4 %copy-start.2 = (bf16[160,16,512]{2,1,0:T(8,128)(2,1)S(1)}, bf16[160,16,512]{2,1,0:T(8,128)(2,1)}, u32[]{:S(2)}) copy-start(bf16[160,16,512]{2,1,0:T(8,128)(2,1)} %gather_fusion.1) | copy-start | bytes 7864324
  615.6 7.7 %copy-start.3 = (bf16[160,16,512]{2,1,0:T(8,128)(2,1)S(1)}, bf16[160,16,512]{2,1,0:T(8,128)(2,1)}, u32[]{:S(2)}) copy-start(bf16[160,16,512]{2,1,0:T(8,128)(2,1)} %get-tuple-element.26) | copy-start | bytes 7864324
  628.1 5.8 copy-start.8
  628.1 7.5 %copy-start.4 = (bf16[16,160,8,64]{3,2,1,0:T(8,128)(2,1)S(1)}, bf16[16,160,8,64]{3,2,1,0:T(8,128)(2,1)}, u32[]{:S(2)}) copy-start(bf16[16,160,8,64]{3,2,1,0:T(8,128)(2,1)} %reshape.329) | copy-start | bytes 7864324
Sparse Core Ops, SparseCore 0:
  489.7 38.6 reduce-scatter.4
  611.6 37.0 reduce-scatter.2
